TPU v7x, 512 devices: a whole 4x8x8 slice. The times are simulated.
512 devices in a mesh: row: 16 (over y, z_hi), col: 32 (over x, z_lo, core).
Axes of the slice: x: 4, y: 8, z: 8 (z_hi: 2, z_lo: 4; z = z_hi * 4 + z_lo), core: 2. Of those that a mesh axis runs over, the one named last changes fastest.
Arguments:
- points: bfloat16 [81920, 128], P(('row', 'col')), may hold values from -6 to 6
- w_in: bfloat16 [128, 1024], replicated, may hold values from -0.5 to 0.5
- w_mid: bfloat16 [1024, 1024], replicated, may hold values from -0.1875 to 0.1875
- w_out: bfloat16 [1024, 32], replicated, may hold values from -0.1875 to 0.1875
- lengthscale: float32 [32], replicated, may hold values from 1 to 10
- probes: bfloat16 [8, 81920], P(None, ('row', 'col')), may hold values from -0.0546875 to 0.0546875
Outputs:
- kv: float32 [8, 81920], P(None, ('row', 'col'))
All inputs are finite; a program needn't handle non-finite values.
Results may differ from a plain program's by a relative error of at most 0.0055.
Values may be sent and summed in bfloat16 or wider, within the bound.
No kernel may reach another device: no remote copies, remote signals or barrier semaphores. Data moves between devices by JAX's collectives and lax.ppermute only.
A program may use at most 64 MiB of HBM per device.

v0:
```python
import jax
import jax.numpy as jnp
from jax import lax
from jax.sharding import PartitionSpec as P


def wide_general(left, right, dims):
    return lax.dot_general(
        left.astype(jnp.float32),
        right.astype(jnp.float32),
        (dims, ((), ())),
        precision=lax.Precision.HIGHEST,
    )


def matern_tile(left_feats, left_sq, right_feats):
    cross_term = wide_general(left_feats, right_feats, ((0,), (0,)))
    right_wide = right_feats.astype(jnp.float32)
    right_sq = jnp.sum(right_wide * right_wide, axis=0)
    dist_sq = jnp.maximum(left_sq[:, None] + right_sq[None, :] - 2.0 * cross_term, 0.0)
    scaled_dist = jnp.sqrt(5.0 * dist_sq)
    values = (1.0 + scaled_dist + scaled_dist * scaled_dist / 3.0) * jnp.exp(-scaled_dist)
    return values.astype(jnp.bfloat16)


def block_width(columns):
    for candidate in (256, 384, 128):
        return candidate
    return columns


def on_device(points, w_in, w_mid, w_out, lengthscale, probes):
    hidden_one = jax.nn.relu(wide_general(points, w_in, ((1,), (0,)))).astype(jnp.bfloat16)
    hidden_two = jax.nn.relu(wide_general(hidden_one, w_mid, ((1,), (0,)))).astype(jnp.bfloat16)
    features = wide_general(w_out, hidden_two, ((0,), (1,)))
    scaled = (features / lengthscale[:, None]).astype(jnp.bfloat16)
    probe_rows = probes.shape[0]
    row_feats = lax.all_gather(scaled, "col", axis=1, tiled=True)
    row_wide = row_feats.astype(jnp.float32)
    row_sq = jnp.sum(row_wide * row_wide, axis=0)
    initial = jnp.zeros((probe_rows, row_feats.shape[1]), jnp.float32)
    piece_feats = lax.all_gather(scaled, "row", axis=1, tiled=True)
    piece_probes = lax.all_gather(probes, "row", axis=1, tiled=True)
    block_cols = block_width(piece_feats.shape[1])

    def advance(position, row_acc):
        column_start = position * block_cols
        feats_block = lax.dynamic_slice_in_dim(piece_feats, column_start, block_cols, 1)
        probes_block = lax.dynamic_slice_in_dim(piece_probes, column_start, block_cols, 1)
        kernel_tile = matern_tile(row_feats, row_sq, feats_block)
        return row_acc + wide_general(probes_block, kernel_tile, ((1,), (1,)))

    folded = lax.fori_loop(0, piece_feats.shape[1] // block_cols, advance, initial)
    column_sums = 0.0
    row_sums = lax.psum_scatter(folded, "col", scatter_dimension=1, tiled=True)
    return row_sums + column_sums


def solution(mesh):
    in_specs = (P(("row", "col"), None), P(), P(), P(), P(), P(None, ("row", "col")))
    out_specs = P(None, ("row", "col"))
    return jax.shard_map(
        on_device, mesh=mesh, in_specs=in_specs, out_specs=out_specs, check_vma=False
    )
```

profile of v0, /device:TPU:8, one launch (start us, length us, event | category | flops | bytes accessed | tf_op | source)
XLA Modules:
  0.0 365.1 jit_solution(8537713413298541568)
XLA Ops:
  6.6 1.3 fusion.9
  8.2 0.5 fusion.10
  9.0 57.5 %all-gather.2 = bf16[16,160,32]{1,2,0:T(8,128)(2,1)S(1)} all-gather(bf16[1,160,32]{1,2,0:T(8,128)(2,1)S(1)} %fusion.12), channel_id=1, replica_groups=mesh['row'=16,'col'=32] {'row'}, dimensions={0}, use_global_device_ids=true | all-gather | bytes 174080 | tf_op jit(solution)/shard_map/all_gather | solution.py:42
  66.5 44.4 %all-gather.1 = bf16[32,160,32]{1,2,0:T(8,128)(2,1)S(1)} all-gather(bf16[1,160,32]{1,2,0:T(8,128)(2,1)S(1)} %fusion.12), channel_id=1, replica_groups=mesh['row'=16,'col'=32] {'col'}, dimensions={0}, use_global_device_ids=true | all-gather | bytes 337920 | tf_op jit(solution)/shard_map/all_gather | solution.py:38
  110.9 45.5 %all-gather = bf16[16,160,8]{1,2,0:T(8,128)(2,1)S(1)} all-gather(bf16[1,160,8]{1,2,0:T(8,128)(2,1)S(1)} %bitcast.48), channel_id=1, replica_groups=mesh['row'=16,'col'=32] {'row'}, dimensions={0}, use_global_device_ids=true | all-gather | bytes 43520 | tf_op jit(solution)/shard_map/all_gather | solution.py:43
  157.3 0.7 reshape.6
  158.2 44.2 %while.14 = (s32[]{:T(128)}, f32[8,5120]{1,0:T(8,128)S(1)}, bf16[8,2560]{1,0:T(8,128)(2,1)S(1)}, f32[5120]{0:T(1024)S(1)}, bf16[32,2560]{1,0:T(8,128)(2,1)S(1)},...) while((s32[]{:T(128)}, f32[8,5120]{1,0:T(8,128)S(1)}, ...), condition=%wide.region_3.4_spmd.clone, body=%wide.region_1.3_spmd.clone.sunk | while | flops 120692488 | bytes 5957809 | solution.py:53
  158.2 3.9 %multiply_convert_fusion.2 = bf16[5120,256]{0,1:T(8,128)(2,1)S(1)} fusion(bf16[32,5120]{1,0:T(8,128)(2,1)S(1)} %get-tuple-element.210, f32[256]{0:T(256)S(1)} %multiply_reduce_fusion.3, f32[5120]{0:T(1024)S(1)} %get-tuple-element.208, bf16[32,2560]{1,0:T(8,128)(2,1)S(1)} %get-tuple-element.209, s32[]{:T(128)S(6)} %select_n.10), kind=kOutput, calls=%fused_computation.7.clone.1 | convolution fusion | flops 99614720 | bytes 2987012 | tf_op jit(solution)/shard_map/while/body/eval_jaxpr/dot_general | solution.py:8
  162.1 0.4 convolution_add_fusion.2
  162.6 3.9 %multiply_convert_fusion.2 = bf16[5120,256]{0,1:T(8,128)(2,1)S(1)} fusion(bf16[32,5120]{1,0:T(8,128)(2,1)S(1)} %get-tuple-element.210, f32[256]{0:T(256)S(1)} %multiply_reduce_fusion.3, f32[5120]{0:T(1024)S(1)} %get-tuple-element.208, bf16[32,2560]{1,0:T(8,128)(2,1)S(1)} %get-tuple-element.209, s32[]{:T(128)S(6)} %select_n.10), kind=kOutput, calls=%fused_computation.7.clone.1 | convolution fusion | flops 99614720 | bytes 2987012 | tf_op jit(solution)/shard_map/while/body/eval_jaxpr/dot_general | solution.py:8
  166.5 0.4 convolution_add_fusion.2
  167.0 3.9 %multiply_convert_fusion.2 = bf16[5120,256]{0,1:T(8,128)(2,1)S(1)} fusion(bf16[32,5120]{1,0:T(8,128)(2,1)S(1)} %get-tuple-element.210, f32[256]{0:T(256)S(1)} %multiply_reduce_fusion.3, f32[5120]{0:T(1024)S(1)} %get-tuple-element.208, bf16[32,2560]{1,0:T(8,128)(2,1)S(1)} %get-tuple-element.209, s32[]{:T(128)S(6)} %select_n.10), kind=kOutput, calls=%fused_computation.7.clone.1 | convolution fusion | flops 99614720 | bytes 2987012 | tf_op jit(solution)/shard_map/while/body/eval_jaxpr/dot_general | solution.py:8
  171.4 3.9 %multiply_convert_fusion.2 = bf16[5120,256]{0,1:T(8,128)(2,1)S(1)} fusion(bf16[32,5120]{1,0:T(8,128)(2,1)S(1)} %get-tuple-element.210, f32[256]{0:T(256)S(1)} %multiply_reduce_fusion.3, f32[5120]{0:T(1024)S(1)} %get-tuple-element.208, bf16[32,2560]{1,0:T(8,128)(2,1)S(1)} %get-tuple-element.209, s32[]{:T(128)S(6)} %select_n.10), kind=kOutput, calls=%fused_computation.7.clone.1 | convolution fusion | flops 99614720 | bytes 2987012 | tf_op jit(solution)/shard_map/while/body/eval_jaxpr/dot_general | solution.py:8
  175.9 3.9 %multiply_convert_fusion.2 = bf16[5120,256]{0,1:T(8,128)(2,1)S(1)} fusion(bf16[32,5120]{1,0:T(8,128)(2,1)S(1)} %get-tuple-element.210, f32[256]{0:T(256)S(1)} %multiply_reduce_fusion.3, f32[5120]{0:T(1024)S(1)} %get-tuple-element.208, bf16[32,2560]{1,0:T(8,128)(2,1)S(1)} %get-tuple-element.209, s32[]{:T(128)S(6)} %select_n.10), kind=kOutput, calls=%fused_computation.7.clone.1 | convolution fusion | flops 99614720 | bytes 2987012 | tf_op jit(solution)/shard_map/while/body/eval_jaxpr/dot_general | solution.py:8
  179.8 0.4 convolution_add_fusion.2
  180.3 3.9 %multiply_convert_fusion.2 = bf16[5120,256]{0,1:T(8,128)(2,1)S(1)} fusion(bf16[32,5120]{1,0:T(8,128)(2,1)S(1)} %get-tuple-element.210, f32[256]{0:T(256)S(1)} %multiply_reduce_fusion.3, f32[5120]{0:T(1024)S(1)} %get-tuple-element.208, bf16[32,2560]{1,0:T(8,128)(2,1)S(1)} %get-tuple-element.209, s32[]{:T(128)S(6)} %select_n.10), kind=kOutput, calls=%fused_computation.7.clone.1 | convolution fusion | flops 99614720 | bytes 2987012 | tf_op jit(solution)/shard_map/while/body/eval_jaxpr/dot_general | solution.py:8
  184.7 3.9 %multiply_convert_fusion.2 = bf16[5120,256]{0,1:T(8,128)(2,1)S(1)} fusion(bf16[32,5120]{1,0:T(8,128)(2,1)S(1)} %get-tuple-element.210, f32[256]{0:T(256)S(1)} %multiply_reduce_fusion.3, f32[5120]{0:T(1024)S(1)} %get-tuple-element.208, bf16[32,2560]{1,0:T(8,128)(2,1)S(1)} %get-tuple-element.209, s32[]{:T(128)S(6)} %select_n.10), kind=kOutput, calls=%fused_computation.7.clone.1 | convolution fusion | flops 99614720 | bytes 2987012 | tf_op jit(solution)/shard_map/while/body/eval_jaxpr/dot_general | solution.py:8
  189.1 3.9 %multiply_convert_fusion.2 = bf16[5120,256]{0,1:T(8,128)(2,1)S(1)} fusion(bf16[32,5120]{1,0:T(8,128)(2,1)S(1)} %get-tuple-element.210, f32[256]{0:T(256)S(1)} %multiply_reduce_fusion.3, f32[5120]{0:T(1024)S(1)} %get-tuple-element.208, bf16[32,2560]{1,0:T(8,128)(2,1)S(1)} %get-tuple-element.209, s32[]{:T(128)S(6)} %select_n.10), kind=kOutput, calls=%fused_computation.7.clone.1 | convolution fusion | flops 99614720 | bytes 2987012 | tf_op jit(solution)/shard_map/while/body/eval_jaxpr/dot_general | solution.py:8
  193.5 3.9 %multiply_convert_fusion.2 = bf16[5120,256]{0,1:T(8,128)(2,1)S(1)} fusion(bf16[32,5120]{1,0:T(8,128)(2,1)S(1)} %get-tuple-element.210, f32[256]{0:T(256)S(1)} %multiply_reduce_fusion.3, f32[5120]{0:T(1024)S(1)} %get-tuple-element.208, bf16[32,2560]{1,0:T(8,128)(2,1)S(1)} %get-tuple-element.209, s32[]{:T(128)S(6)} %select_n.10), kind=kOutput, calls=%fused_computation.7.clone.1 | convolution fusion | flops 99614720 | bytes 2987012 | tf_op jit(solution)/shard_map/while/body/eval_jaxpr/dot_general | solution.py:8
  197.5 0.4 convolution_add_fusion.2
  198.0 3.9 %multiply_convert_fusion.2 = bf16[5120,256]{0,1:T(8,128)(2,1)S(1)} fusion(bf16[32,5120]{1,0:T(8,128)(2,1)S(1)} %get-tuple-element.210, f32[256]{0:T(256)S(1)} %multiply_reduce_fusion.3, f32[5120]{0:T(1024)S(1)} %get-tuple-element.208, bf16[32,2560]{1,0:T(8,128)(2,1)S(1)} %get-tuple-element.209, s32[]{:T(128)S(6)} %select_n.10), kind=kOutput, calls=%fused_computation.7.clone.1 | convolution fusion | flops 99614720 | bytes 2987012 | tf_op jit(solution)/shard_map/while/body/eval_jaxpr/dot_general | solution.py:8
  202.3 2.3 copy.16
  204.6 152.1 %reduce-scatter.4.cloned.1.call-done = f32[160,8]{1,0:T(8,128)} async-done(((f32[5120,8]{1,0:T(8,128)}), f32[160,8]{1,0:T(8,128)}) %reduce-scatter.4.cloned.1.call-update) | async-done | bytes 5136
  356.7 1.6 copy.17
  (34 shorter events, 4.5 us)
Async XLA Ops:
  6.5 1.7 copy-start
  6.5 2.2 copy-start.3
  6.5 2.2 copy-start.2
  6.5 104.3 %copy-start.1 = (bf16[8,160]{1,0:T(8,128)(2,1)S(1)}, bf16[8,160]{1,0:T(8,128)(2,1)}, u32[]{:S(2)}) copy-start(bf16[8,160]{1,0:T(8,128)(2,1)} %param.13) | copy-start | bytes 7684
  6.5 350.2 %reduce-scatter.4.cloned.1.call-start = ((), (), s32[]{:S(2)}) async-start(), calls=%async_computation.1 | async-start | bytes 2703360
Sparse Core Ops, SparseCore 0:
  204.7 151.9 reduce-scatter.3
where the time goes:
time: 365 us
  waiting for transfers between devices  152 us (42%)
  blocking collectives  147 us (40%)
  matrix products  45.8 us (13%)
  between operations  13.5 us (4%)
  local copies, waits for them, and re-layouts  5.77 us (2%)
    unnamed x2, waiting for transfers between devices  152 us
    all_gather x1, blocking collectives, on_device(): piece_feats = lax.all_gather(scaled, 'row', axis=1, tiled=True)  57.5 us
    dot_general x23, matrix products, wide_general(): lax.dot_general(left.astype(jnp.float32), right.astype(jnp.float32), (dim...  45.8 us
    all_gather x1, blocking collectives, on_device(): piece_probes = lax.all_gather(probes, 'row', axis=1, tiled=True)  45.5 us
    all_gather x1, blocking collectives, on_device(): row_feats = lax.all_gather(scaled, 'col', axis=1, tiled=True)  44.4 us
  transfers between devices with their start and end apart: 1, of which 1 were waited for; matrix products, arithmetic and copies ran while one was open for 0% of the time, Pallas kernels for 0%

commit v1 on v0

--- a/solution.py
+++ b/solution.py
@@ -35,7 +35,10 @@
     features = wide_general(w_out, hidden_two, ((0,), (1,)))
     scaled = (features / lengthscale[:, None]).astype(jnp.bfloat16)
     probe_rows = probes.shape[0]
-    row_feats = lax.all_gather(scaled, "col", axis=1, tiled=True)
+    size = lax.axis_size("col")
+    pieces = jnp.stack([scaled for _ in range(size)])
+    pieces = lax.all_to_all(pieces, "col", split_axis=0, concat_axis=0)
+    row_feats = jnp.concatenate(pieces, axis=1)
     row_wide = row_feats.astype(jnp.float32)
     row_sq = jnp.sum(row_wide * row_wide, axis=0)
     initial = jnp.zeros((probe_rows, row_feats.shape[1]), jnp.float32)

time: 365 us -> 334 us (0.915)
  the two profiles are of different devices: /device:TPU:8 before, /device:TPU:24 now
where the time goes in v1:
time: 334 us
  waiting for transfers between devices  154 us (46%)
  blocking collectives  103 us (31%)
  matrix products  45.8 us (14%)
  between operations  13.5 us (4%)
  starting transfers between devices  10.2 us (3%)
  local copies, waits for them, and re-layouts  6.75 us (2%)
    unnamed x2, waiting for transfers between devices  154 us
    all_gather x1, blocking collectives, on_device(): piece_feats = lax.all_gather(scaled, 'row', axis=1, tiled=True)  51.8 us
    all_gather x1, blocking collectives, on_device(): piece_probes = lax.all_gather(probes, 'row', axis=1, tiled=True)  51.3 us
    dot_general x23, matrix products, wide_general(): lax.dot_general(left.astype(jnp.float32), right.astype(jnp.float32), (dim...  45.8 us
    all_to_all x1, starting transfers between devices, on_device(): pieces = lax.all_to_all(pieces, 'col', split_axis=0, concat_axis=0)  10.1 us
  transfers between devices with their start and end apart: 2, of which 1 were waited for; matrix products, arithmetic and copies ran while one was open for 0% of the time, Pallas kernels for 0%

profile of v1, /device:TPU:24, one launch (start us, length us, event | category | flops | bytes accessed | tf_op | source)
XLA Modules:
  0.0 333.9 jit_solution(13572845322661566989)
XLA Ops:
  6.5 1.4 fusion.9
  8.2 0.5 fusion.10
  9.0 0.8 stack.2
  9.8 10.1 %all-to-all-start = ((bf16[32,32,160]{2,1,0:T(8,128)(2,1)}), bf16[32,32,160]{2,1,0:T(8,128)(2,1)S(1)}, u32[]{:S(2)}, u32[]{:S(2)}) async-start(bf16[32,32,160]{2,1,0:T(8,128)(2,1)} %stack.2), calls=%async_computation | async-start | bytes 1048576 | tf_op jit(solution)/shard_map/all_to_all | solution.py:40
  20.0 51.3 %all-gather = bf16[16,160,8]{1,2,0:T(8,128)(2,1)S(1)} all-gather(bf16[1,160,8]{1,2,0:T(8,128)(2,1)S(1)} %bitcast.48), channel_id=1, replica_groups=mesh['row'=16,'col'=32] {'row'}, dimensions={0}, use_global_device_ids=true | all-gather | bytes 43520 | tf_op jit(solution)/shard_map/all_gather | solution.py:46
  71.5 51.8 %all-gather.1 = bf16[16,160,32]{1,2,0:T(8,128)(2,1)S(1)} all-gather(bf16[1,160,32]{1,2,0:T(8,128)(2,1)S(1)} %bitcast.47), channel_id=1, replica_groups=mesh['row'=16,'col'=32] {'row'}, dimensions={0}, use_global_device_ids=true | all-gather | bytes 174080 | tf_op jit(solution)/shard_map/all_gather | solution.py:45
  124.3 0.7 reshape.13
  125.1 44.2 %while.14 = (s32[]{:T(128)}, f32[8,5120]{1,0:T(8,128)S(1)}, bf16[8,2560]{1,0:T(8,128)(2,1)S(1)}, f32[5120]{0:T(1024)S(1)}, bf16[32,2560]{1,0:T(8,128)(2,1)S(1)},...) while((s32[]{:T(128)}, f32[8,5120]{1,0:T(8,128)S(1)}, ...), condition=%wide.region_3.4_spmd.clone, body=%wide.region_1.3_spmd.clone.sunk | while | flops 120692488 | bytes 5957809 | solution.py:56
  125.1 3.9 %multiply_convert_fusion.2 = bf16[5120,256]{0,1:T(8,128)(2,1)S(1)} fusion(bf16[32,5120]{1,0:T(8,128)(2,1)S(1)} %get-tuple-element.210, f32[256]{0:T(256)S(1)} %multiply_reduce_fusion.3, f32[5120]{0:T(1024)S(1)} %get-tuple-element.208, bf16[32,2560]{1,0:T(8,128)(2,1)S(1)} %get-tuple-element.209, s32[]{:T(128)S(6)} %select_n.10), kind=kOutput, calls=%fused_computation.7.clone.1 | convolution fusion | flops 99614720 | bytes 2987012 | tf_op jit(solution)/shard_map/while/body/eval_jaxpr/dot_general | solution.py:8
  129.1 0.4 convolution_add_fusion.2
  129.5 3.9 %multiply_convert_fusion.2 = bf16[5120,256]{0,1:T(8,128)(2,1)S(1)} fusion(bf16[32,5120]{1,0:T(8,128)(2,1)S(1)} %get-tuple-element.210, f32[256]{0:T(256)S(1)} %multiply_reduce_fusion.3, f32[5120]{0:T(1024)S(1)} %get-tuple-element.208, bf16[32,2560]{1,0:T(8,128)(2,1)S(1)} %get-tuple-element.209, s32[]{:T(128)S(6)} %select_n.10), kind=kOutput, calls=%fused_computation.7.clone.1 | convolution fusion | flops 99614720 | bytes 2987012 | tf_op jit(solution)/shard_map/while/body/eval_jaxpr/dot_general | solution.py:8
  134.0 3.9 %multiply_convert_fusion.2 = bf16[5120,256]{0,1:T(8,128)(2,1)S(1)} fusion(bf16[32,5120]{1,0:T(8,128)(2,1)S(1)} %get-tuple-element.210, f32[256]{0:T(256)S(1)} %multiply_reduce_fusion.3, f32[5120]{0:T(1024)S(1)} %get-tuple-element.208, bf16[32,2560]{1,0:T(8,128)(2,1)S(1)} %get-tuple-element.209, s32[]{:T(128)S(6)} %select_n.10), kind=kOutput, calls=%fused_computation.7.clone.1 | convolution fusion | flops 99614720 | bytes 2987012 | tf_op jit(solution)/shard_map/while/body/eval_jaxpr/dot_general | solution.py:8
  138.4 3.9 %multiply_convert_fusion.2 = bf16[5120,256]{0,1:T(8,128)(2,1)S(1)} fusion(bf16[32,5120]{1,0:T(8,128)(2,1)S(1)} %get-tuple-element.210, f32[256]{0:T(256)S(1)} %multiply_reduce_fusion.3, f32[5120]{0:T(1024)S(1)} %get-tuple-element.208, bf16[32,2560]{1,0:T(8,128)(2,1)S(1)} %get-tuple-element.209, s32[]{:T(128)S(6)} %select_n.10), kind=kOutput, calls=%fused_computation.7.clone.1 | convolution fusion | flops 99614720 | bytes 2987012 | tf_op jit(solution)/shard_map/while/body/eval_jaxpr/dot_general | solution.py:8
  142.8 3.9 %multiply_convert_fusion.2 = bf16[5120,256]{0,1:T(8,128)(2,1)S(1)} fusion(bf16[32,5120]{1,0:T(8,128)(2,1)S(1)} %get-tuple-element.210, f32[256]{0:T(256)S(1)} %multiply_reduce_fusion.3, f32[5120]{0:T(1024)S(1)} %get-tuple-element.208, bf16[32,2560]{1,0:T(8,128)(2,1)S(1)} %get-tuple-element.209, s32[]{:T(128)S(6)} %select_n.10), kind=kOutput, calls=%fused_computation.7.clone.1 | convolution fusion | flops 99614720 | bytes 2987012 | tf_op jit(solution)/shard_map/while/body/eval_jaxpr/dot_general | solution.py:8
  146.7 0.4 convolution_add_fusion.2
  147.2 3.9 %multiply_convert_fusion.2 = bf16[5120,256]{0,1:T(8,128)(2,1)S(1)} fusion(bf16[32,5120]{1,0:T(8,128)(2,1)S(1)} %get-tuple-element.210, f32[256]{0:T(256)S(1)} %multiply_reduce_fusion.3, f32[5120]{0:T(1024)S(1)} %get-tuple-element.208, bf16[32,2560]{1,0:T(8,128)(2,1)S(1)} %get-tuple-element.209, s32[]{:T(128)S(6)} %select_n.10), kind=kOutput, calls=%fused_computation.7.clone.1 | convolution fusion | flops 99614720 | bytes 2987012 | tf_op jit(solution)/shard_map/while/body/eval_jaxpr/dot_general | solution.py:8
  151.6 3.9 %multiply_convert_fusion.2 = bf16[5120,256]{0,1:T(8,128)(2,1)S(1)} fusion(bf16[32,5120]{1,0:T(8,128)(2,1)S(1)} %get-tuple-element.210, f32[256]{0:T(256)S(1)} %multiply_reduce_fusion.3, f32[5120]{0:T(1024)S(1)} %get-tuple-element.208, bf16[32,2560]{1,0:T(8,128)(2,1)S(1)} %get-tuple-element.209, s32[]{:T(128)S(6)} %select_n.10), kind=kOutput, calls=%fused_computation.7.clone.1 | convolution fusion | flops 99614720 | bytes 2987012 | tf_op jit(solution)/shard_map/while/body/eval_jaxpr/dot_general | solution.py:8
  156.1 3.9 %multiply_convert_fusion.2 = bf16[5120,256]{0,1:T(8,128)(2,1)S(1)} fusion(bf16[32,5120]{1,0:T(8,128)(2,1)S(1)} %get-tuple-element.210, f32[256]{0:T(256)S(1)} %multiply_reduce_fusion.3, f32[5120]{0:T(1024)S(1)} %get-tuple-element.208, bf16[32,2560]{1,0:T(8,128)(2,1)S(1)} %get-tuple-element.209, s32[]{:T(128)S(6)} %select_n.10), kind=kOutput, calls=%fused_computation.7.clone.1 | convolution fusion | flops 99614720 | bytes 2987012 | tf_op jit(solution)/shard_map/while/body/eval_jaxpr/dot_general | solution.py:8
  160.5 3.9 %multiply_convert_fusion.2 = bf16[5120,256]{0,1:T(8,128)(2,1)S(1)} fusion(bf16[32,5120]{1,0:T(8,128)(2,1)S(1)} %get-tuple-element.210, f32[256]{0:T(256)S(1)} %multiply_reduce_fusion.3, f32[5120]{0:T(1024)S(1)} %get-tuple-element.208, bf16[32,2560]{1,0:T(8,128)(2,1)S(1)} %get-tuple-element.209, s32[]{:T(128)S(6)} %select_n.10), kind=kOutput, calls=%fused_computation.7.clone.1 | convolution fusion | flops 99614720 | bytes 2987012 | tf_op jit(solution)/shard_map/while/body/eval_jaxpr/dot_general | solution.py:8
  164.4 0.4 convolution_add_fusion.2
  164.9 3.9 %multiply_convert_fusion.2 = bf16[5120,256]{0,1:T(8,128)(2,1)S(1)} fusion(bf16[32,5120]{1,0:T(8,128)(2,1)S(1)} %get-tuple-element.210, f32[256]{0:T(256)S(1)} %multiply_reduce_fusion.3, f32[5120]{0:T(1024)S(1)} %get-tuple-element.208, bf16[32,2560]{1,0:T(8,128)(2,1)S(1)} %get-tuple-element.209, s32[]{:T(128)S(6)} %select_n.10), kind=kOutput, calls=%fused_computation.7.clone.1 | convolution fusion | flops 99614720 | bytes 2987012 | tf_op jit(solution)/shard_map/while/body/eval_jaxpr/dot_general | solution.py:8
  169.3 2.3 copy.14
  171.6 153.9 %reduce-scatter.4.cloned.1.call-done = f32[160,8]{1,0:T(8,128)} async-done(((f32[5120,8]{1,0:T(8,128)}), f32[160,8]{1,0:T(8,128)}) %reduce-scatter.4.cloned.1.call-update) | async-done | bytes 5136
  325.5 1.6 copy.15
  (37 shorter events, 5.2 us)
Async XLA Ops:
  6.5 1.7 copy-start
  6.5 2.2 copy-start.3
  6.5 2.2 copy-start.2
  6.5 13.5 %copy-start.1 = (bf16[8,160]{1,0:T(8,128)(2,1)S(1)}, bf16[8,160]{1,0:T(8,128)(2,1)}, u32[]{:S(2)}) copy-start(bf16[8,160]{1,0:T(8,128)(2,1)} %param.13) | copy-start | bytes 7684
  9.8 113.9 %all-to-all-start = ((bf16[32,32,160]{2,1,0:T(8,128)(2,1)}), bf16[32,32,160]{2,1,0:T(8,128)(2,1)S(1)}, u32[]{:S(2)}, u32[]{:S(2)}) async-start(bf16[32,32,160]{2,1,0:T(8,128)(2,1)} %stack.2), calls=%async_computation | async-start | bytes 1048576 | tf_op jit(solution)/shard_map/all_to_all | solution.py:40
  20.0 305.5 %reduce-scatter.4.cloned.1.call-start = ((), (), s32[]{:S(2)}) async-start(), calls=%async_computation.2 | async-start | bytes 2703360
Sparse Core Ops, SparseCore 0:
  171.7 153.7 reduce-scatter.3
